TPU v7x, 32 devices: a whole 2x2x4 slice. The times are simulated.
32 devices in a mesh: occ: 4 (over z), aux: 4 (over x, core), vir: 2 (over y).
Axes of the slice: x: 2, y: 2, z: 4, core: 2. Of those that a mesh axis runs over, the one named last changes fastest.
Arguments:
- integrals: bfloat16 [4, 2048, 4096], P('occ', 'vir', 'aux'), may hold values from -0.65625 to 0.65625
- occ_energy: float32 [4], replicated, may hold values from -2 to -0.5
- vir_energy: float32 [2048], replicated, may hold values from 0.25 to 3
Outputs:
- lagrangian: bfloat16 [4, 2048, 4096], P('occ', 'vir', 'aux')
All inputs are finite; a program needn't handle non-finite values.
Results may differ from a plain program's by a relative error of at most 0.0039.
Values may be sent and summed in bfloat16 or wider, within the bound.
No kernel may reach another device: no remote copies, remote signals or barrier semaphores. Data moves between devices by JAX's collectives and lax.ppermute only.
A program may use at most 64 MiB of HBM per device.

v0:
```python
import jax
import jax.numpy as jnp
from jax import lax
from jax.sharding import PartitionSpec as P

CHUNKS = 4
AUX_BY_PERMUTE = False
Z_GATED = False


def shifted_2(value, axis, by):
    count = lax.axis_size(axis)
    return lax.ppermute(value, axis, [(i, (i + by) % count) for i in range(count)])


def general_plan(integrals, occ_energy, vir_energy):
    row_count = integrals.shape[0]
    vir_width = integrals.shape[1]
    cycle_size = lax.axis_size("occ")
    position = lax.axis_index("occ")
    own_level = lax.dynamic_slice_in_dim(occ_energy, position * row_count, row_count)
    partner_level = lax.dynamic_slice_in_dim(
        occ_energy, (position - 2) % cycle_size * row_count, row_count
    )
    local_vir = lax.dynamic_slice_in_dim(vir_energy, lax.axis_index("vir") * vir_width, vir_width)
    shifted = shifted_2(integrals, "occ", 2)
    partner = lax.all_gather(shifted, "vir", axis=1, tiled=True)
    virtuals = partner.shape[1]
    pair_level = own_level + partner_level
    share_rows = virtuals // lax.axis_size("aux")
    partial_value = lax.psum_scatter(
        jnp.einsum("nbq,naq->bna", partner, integrals, preferred_element_type=jnp.float32),
        "aux",
        scatter_dimension=0,
        tiled=True,
    )
    first_row = lax.axis_index("aux") * share_rows
    vir_rows = lax.dynamic_slice_in_dim(vir_energy, first_row, share_rows)
    amplitudes = (
        partial_value
        / (pair_level[None, :, None] - vir_rows[:, None, None] - local_vir[None, None, :])
    ).astype(jnp.bfloat16)
    portion = lax.all_gather(amplitudes, "aux", axis=0, tiled=True)
    own_part = jnp.einsum("bna,nbq->naq", portion, partner, preferred_element_type=jnp.float32)
    rows_back = jnp.einsum("bna,naq->nbq", portion, integrals, preferred_element_type=jnp.float32)
    owned = lax.psum_scatter(rows_back, "vir", scatter_dimension=1, tiled=True)
    returned = shifted_2(owned, "occ", -2)
    return (own_part + returned).astype(jnp.bfloat16)


def xor_pairs(count, step):
    return [(j, j ^ step) for j in range(count)]


def aux_reduce_scatter(x):
    count = lax.axis_size("aux")
    k = lax.axis_index("aux")
    first = 0
    step = 1
    while step < count:
        half = x.shape[0] // 2
        bit = k // step % 2
        keep = lax.dynamic_slice_in_dim(x, bit * half, half, 0)
        send = lax.dynamic_slice_in_dim(x, (1 - bit) * half, half, 0)
        x = keep + lax.ppermute(send, "aux", xor_pairs(count, step))
        first = first + bit * half
        step *= 2
    return (x, first)


def aux_all_gather(x):
    count = lax.axis_size("aux")
    k = lax.axis_index("aux")
    step = count // 2
    while step >= 1:
        bit = k // step % 2
        other = lax.ppermute(x, "aux", xor_pairs(count, step))
        x = jnp.where(bit == 0, jnp.concatenate([x, other]), jnp.concatenate([other, x]))
        step //= 2
    return x


def paired_plan(integrals, occ_energy, vir_energy):
    own = integrals[0]
    vir_rows, _ = own.shape
    cycle_size = lax.axis_size("occ")
    position = lax.axis_index("occ")
    pair_level = occ_energy[position] + occ_energy[(position - 2) % cycle_size]
    vir_pos = lax.axis_index("vir")
    vir_count = lax.axis_size("vir")
    aux_count = lax.axis_size("aux")
    share = vir_rows // aux_count
    width = vir_rows // CHUNKS
    if not AUX_BY_PERMUTE:
        first_row = lax.axis_index("aux") * share

    def forward(c, arrived):
        if vir_count == 2:
            mate = shifted_2(arrived, "vir", 1)
            block = jnp.concatenate([arrived, mate])
            cols = [vir_pos, 1 - vir_pos]
        else:
            block = lax.all_gather(arrived, "vir", axis=0, tiled=True)
            cols = list(range(vir_count))
        col_level = jnp.concatenate(
            [lax.dynamic_slice_in_dim(vir_energy, w * vir_rows + c * width, width) for w in cols]
        )
        return (block, col_level)

    def reduce(block):
        partial = jnp.einsum("aq,bq->ab", own, block, preferred_element_type=jnp.float32)
        if AUX_BY_PERMUTE:
            return aux_reduce_scatter(partial)
        return (lax.psum_scatter(partial, "aux", scatter_dimension=0, tiled=True), first_row)

    def amplitudes_of(summed, first, col_level):
        row_level = lax.dynamic_slice_in_dim(vir_energy, vir_pos * vir_rows + first, share)
        amplitudes = (summed / (pair_level - row_level[:, None] - col_level[None, :])).astype(
            jnp.bfloat16
        )
        if AUX_BY_PERMUTE:
            return aux_all_gather(amplitudes)
        return lax.all_gather(amplitudes, "aux", axis=0, tiled=True)

    arrived = [None] * CHUNKS
    blocks = [None] * CHUNKS
    levels = [None] * CHUNKS
    summed = [None] * CHUNKS
    firsts = [None] * CHUNKS
    gathered = [None] * CHUNKS
    total = None
    for c in range(CHUNKS if not Z_GATED else 0):
        arrived[c] = shifted_2(own[c * width : (c + 1) * width], "occ", 2)
    for t in range(CHUNKS + 4):
        piece = own[t * width : (t + 1) * width] if Z_GATED and t < CHUNKS else None
        if t > 0:
            gate = {"arrived": arrived[t - 1] if t - 1 < CHUNKS else None}
            if piece is not None:
                gate["piece"] = piece
            if 0 <= t - 2 < CHUNKS:
                gate["block"] = blocks[t - 2]
            if 0 <= t - 3 < CHUNKS:
                gate["summed"] = summed[t - 3]
            if 0 <= t - 4 < CHUNKS:
                gate["gathered"] = gathered[t - 4]
            if total is not None:
                gate["total"] = total
            gate = lax.optimization_barrier(gate)
            if piece is not None:
                piece = gate["piece"]
            if t - 1 < CHUNKS:
                arrived[t - 1] = gate["arrived"]
            if 0 <= t - 2 < CHUNKS:
                blocks[t - 2] = gate["block"]
            if 0 <= t - 3 < CHUNKS:
                summed[t - 3] = gate["summed"]
            if 0 <= t - 4 < CHUNKS:
                gathered[t - 4] = gate["gathered"]
            if total is not None:
                total = gate["total"]
        if piece is not None:
            arrived[t] = shifted_2(piece, "occ", 2)
        c = t - 1
        if 0 <= c < CHUNKS:
            blocks[c], levels[c] = forward(c, arrived[c])
        c = t - 2
        if 0 <= c < CHUNKS:
            summed[c], firsts[c] = reduce(blocks[c])
        c = t - 3
        if 0 <= c < CHUNKS:
            gathered[c] = amplitudes_of(summed[c], firsts[c], levels[c])
        c = t - 4
        if 0 <= c < CHUNKS:
            term = jnp.dot(gathered[c], blocks[c], preferred_element_type=jnp.float32)
            total = term if total is None else total + term
    gamma_own = total
    gamma_back = total
    return (gamma_own + gamma_back).astype(jnp.bfloat16)[None]


def on_device(integrals, occ_energy, vir_energy):
    cycle_size = lax.axis_size("occ")
    if integrals.shape[0] == 1 and 4 % cycle_size == 0 and (integrals.shape[1] % (CHUNKS * 8) == 0):
        return paired_plan(integrals, occ_energy, vir_energy)
    return general_plan(integrals, occ_energy, vir_energy)


def solution(mesh):
    placed = (P("occ", "vir", "aux"), P(), P())
    return jax.shard_map(
        on_device, mesh=mesh, in_specs=placed, out_specs=P("occ", "vir", "aux"), check_vma=False
    )
```

profile of v0, /device:TPU:0, one launch (start us, length us, event | category | flops | bytes accessed | tf_op | source)
XLA Modules:
  0.0 284.6 jit_solution(10130402411361232367)
XLA Ops:
  6.5 2.7 slice_bitcast_fusion
  9.2 4.0 %collective-permute-start.3 = (bf16[256,1024]{1,0:T(8,128)(2,1)S(1)}, bf16[256,1024]{1,0:T(8,128)(2,1)S(1)}, u32[]{:S(2)}, u32[]{:S(2)}) collective-permute-start(bf16[256,1024]{1,0:T(8,128)(2,1)S(1)} %get-tuple-element.41), channel_id=1, source_target_pairs={{0,16},{8,24},{16,0},{24,8},{1,17},{9,25},{17,1},{25,9},{2,18},{10... | collective-permute-start | bytes 1572872 | tf_op jit(solution)/shard_map/ppermute | solution.py:13
  13.3 23.2 %collective-permute-done.3 = bf16[256,1024]{1,0:T(8,128)(2,1)S(1)} collective-permute-done((bf16[256,1024]{1,0:T(8,128)(2,1)S(1)}, bf16[256,1024]{1,0:T(8,128)(2,1)S(1)}, u32[]{:S(2)}, u32[]{:S(2)}) %collective-permute-start.3) | collective-permute-done | bytes 524320 | tf_op jit(solution)/shard_map/ppermute | solution.py:13
  36.4 1.6 collective-permute-start.4
  38.0 11.5 %collective-permute-done.4 = bf16[256,1024]{1,0:T(8,128)(2,1)S(1)} collective-permute-done((bf16[256,1024]{1,0:T(8,128)(2,1)S(1)}, bf16[256,1024]{1,0:T(8,128)(2,1)S(1)}, u32[]{:S(2)}, u32[]{:S(2)}) %collective-permute-start.4) | collective-permute-done | bytes 524320 | tf_op jit(solution)/shard_map/ppermute | solution.py:13
  49.6 13.1 %collective-permute-done.2 = bf16[256,1024]{1,0:T(8,128)(2,1)S(1)} collective-permute-done((bf16[256,1024]{1,0:T(8,128)(2,1)S(1)}, bf16[256,1024]{1,0:T(8,128)(2,1)S(1)}, u32[]{:S(2)}, u32[]{:S(2)}) %collective-permute-start.2) | collective-permute-done | bytes 524320 | tf_op jit(solution)/shard_map/ppermute | solution.py:13
  62.7 2.6 fusion.8
  68.2 9.3 %collective-permute-done.5 = bf16[256,1024]{1,0:T(8,128)(2,1)} collective-permute-done((bf16[256,1024]{1,0:T(8,128)(2,1)S(1)}, bf16[256,1024]{1,0:T(8,128)(2,1)}, u32[]{:S(2)}, u32[]{:S(2)}) %collective-permute-start.5) | collective-permute-done | bytes 524320 | tf_op jit(solution)/shard_map/ppermute | solution.py:13
  78.5 11.8 %collective-permute-done.1 = bf16[256,1024]{1,0:T(8,128)(2,1)S(1)} collective-permute-done((bf16[256,1024]{1,0:T(8,128)(2,1)}, bf16[256,1024]{1,0:T(8,128)(2,1)S(1)}, u32[]{:S(2)}, u32[]{:S(2)}) %collective-permute-start.1) | collective-permute-done | bytes 524320 | tf_op jit(solution)/shard_map/ppermute | solution.py:13
  90.4 4.3 %reduce-scatter.5.cloned.1.call-done = f32[256,512]{0,1:T(8,128)} async-done(((f32[1024,512]{0,1:T(8,128)}), f32[256,512]{0,1:T(8,128)}) %reduce-scatter.5.cloned.1.call-update) | async-done | bytes 524304 | tf_op jit(solution)/shard_map/reduce_scatter | solution.py:114
  94.7 1.9 divide_convert_fusion.3
  96.7 4.2 %fusion.11 = f32[1024,512]{0,1:T(8,128)} fusion(bf16[512,1024]{1,0:T(8,128)(2,1)S(1)} %pad_maximum_fusion.1, bf16[1,1024,1024]{2,1,0:T(8,128)(2,1)} %param.3), kind=kOutput, calls=%fused_computation.11 | convolution fusion | flops 1073741824 | bytes 5242880 | tf_op jit(solution)/shard_map/aq,bq->ab/dot_general | solution.py:111
  101.0 1.6 collective-permute-start.6
  102.5 2.4 collective-permute-start
  104.9 9.8 %collective-permute-done.6 = bf16[256,1024]{1,0:T(8,128)(2,1)S(1)} collective-permute-done((bf16[256,1024]{1,0:T(8,128)(2,1)S(1)}, bf16[256,1024]{1,0:T(8,128)(2,1)S(1)}, u32[]{:S(2)}, u32[]{:S(2)}) %collective-permute-start.6) | collective-permute-done | bytes 524320 | tf_op jit(solution)/shard_map/ppermute | solution.py:13
  115.8 12.5 %collective-permute-done = bf16[256,1024]{1,0:T(8,128)(2,1)} collective-permute-done((bf16[256,1024]{1,0:T(8,128)(2,1)}, bf16[256,1024]{1,0:T(8,128)(2,1)}, u32[]{:S(2)}, u32[]{:S(2)}) %collective-permute-start) | collective-permute-done | bytes 524320 | tf_op jit(solution)/shard_map/ppermute | solution.py:13
  128.4 19.4 %reduce-scatter.7.cloned.1.call-done = f32[256,512]{0,1:T(8,128)} async-done(((f32[1024,512]{0,1:T(8,128)}), f32[256,512]{0,1:T(8,128)}) %reduce-scatter.7.cloned.1.call-update) | async-done | bytes 524304 | tf_op jit(solution)/shard_map/reduce_scatter | solution.py:114
  147.8 1.9 divide_convert_fusion.2
  149.8 4.2 %fusion.14 = f32[1024,512]{0,1:T(8,128)} fusion(bf16[512,1024]{1,0:T(8,128)(2,1)S(1)} %pad_maximum_fusion.2, bf16[1,1024,1024]{2,1,0:T(8,128)(2,1)} %param.3), kind=kOutput, calls=%fused_computation.12 | convolution fusion | flops 1073741824 | bytes 5242880 | tf_op jit(solution)/shard_map/aq,bq->ab/dot_general | solution.py:111
  154.0 1.5 collective-permute-start.7
  155.6 4.5 %fusion.23 = f32[1024,1024]{1,0:T(8,128)} fusion(bf16[1024,512]{0,1:T(8,128)(2,1)} %all-gather.5.cloned.1.call-done, bf16[512,1024]{1,0:T(8,128)(2,1)S(1)} %pad_maximum_fusion), kind=kOutput, calls=%fused_computation.34 | convolution fusion | flops 1073741824 | bytes 6291456 | tf_op jit(solution)/shard_map/dot_general | solution.py:174
  160.1 7.9 %collective-permute-done.7 = bf16[256,1024]{1,0:T(8,128)(2,1)S(1)} collective-permute-done((bf16[256,1024]{1,0:T(8,128)(2,1)}, bf16[256,1024]{1,0:T(8,128)(2,1)S(1)}, u32[]{:S(2)}, u32[]{:S(2)}) %collective-permute-start.7) | collective-permute-done | bytes 524320 | tf_op jit(solution)/shard_map/ppermute | solution.py:13
  169.1 31.4 %reduce-scatter.9.cloned.1.call-done = f32[256,512]{0,1:T(8,128)} async-done(((f32[1024,512]{0,1:T(8,128)}), f32[256,512]{0,1:T(8,128)}) %reduce-scatter.9.cloned.1.call-update) | async-done | bytes 524304 | tf_op jit(solution)/shard_map/reduce_scatter | solution.py:114
  200.6 1.9 divide_convert_fusion.1
  202.6 4.2 %fusion.17 = f32[1024,512]{0,1:T(8,128)} fusion(bf16[512,1024]{1,0:T(8,128)(2,1)S(1)} %pad_maximum_fusion.3, bf16[1,1024,1024]{2,1,0:T(8,128)(2,1)} %param.3), kind=kOutput, calls=%fused_computation.13 | convolution fusion | flops 1073741824 | bytes 5242880 | tf_op jit(solution)/shard_map/aq,bq->ab/dot_general | solution.py:111
  210.3 2.9 %add.120 = f32[1024,1024]{1,0:T(8,128)} add(f32[1024,1024]{1,0:T(8,128)S(1)} %copy-done, f32[1024,1024]{1,0:T(8,128)S(1)} %fusion.24) | non-fusion elementwise | flops 1048576 | bytes 12582912 | tf_op jit(solution)/shard_map/add | solution.py:175
  213.2 6.3 %all-gather.9.cloned.1.call-done = bf16[1024,512]{0,1:T(8,128)(2,1)} async-done(((bf16[256,512]{0,1:T(8,128)(2,1)}), bf16[1024,512]{0,1:T(8,128)(2,1)}) %all-gather.9.cloned.1.call-update) | async-done | bytes 1048592 | tf_op jit(solution)/shard_map/all_gather | solution.py:123
  219.5 34.1 %reduce-scatter.11.cloned.1.call-done = f32[256,512]{0,1:T(8,128)} async-done(((f32[1024,512]{0,1:T(8,128)}), f32[256,512]{0,1:T(8,128)}) %reduce-scatter.11.cloned.1.call-update) | async-done | bytes 524304 | tf_op jit(solution)/shard_map/reduce_scatter | solution.py:114
  253.7 1.9 divide_convert_fusion
  255.6 5.5 %convolution_add_fusion = f32[1024,1024]{1,0:T(8,128)} fusion(f32[1024,1024]{1,0:T(8,128)} %add.120, bf16[1024,512]{0,1:T(8,128)(2,1)S(1)} %copy-done.1, bf16[512,1024]{1,0:T(8,128)(2,1)S(1)} %pad_maximum_fusion.2), kind=kOutput, calls=%fused_computation.1 | convolution fusion | flops 1074790400 | bytes 10485760 | tf_op jit(solution)/shard_map/dot_general | solution.py:174
  261.1 11.5 %all-gather.11.cloned.1.call-done = bf16[1024,512]{0,1:T(8,128)(2,1)} async-done(((bf16[256,512]{0,1:T(8,128)(2,1)}), bf16[1024,512]{0,1:T(8,128)(2,1)}) %all-gather.11.cloned.1.call-update) | async-done | bytes 1048592 | tf_op jit(solution)/shard_map/all_gather | solution.py:123
  272.6 5.1 %fusion.20 = bf16[1,1024,1024]{2,1,0:T(8,128)(2,1)} fusion(f32[1024,1024]{1,0:T(8,128)} %convolution_add_fusion, bf16[1024,512]{0,1:T(8,128)(2,1)} %all-gather.11.cloned.1.call-done, bf16[512,1024]{1,0:T(8,128)(2,1)S(1)} %copy-done.5), kind=kOutput, calls=%fused_computation.14 | convolution fusion | flops 1076887552 | bytes 8388608 | tf_op jit(solution)/shard_map/dot_general | solution.py:174
  (50 shorter events, 8.9 us)
Async XLA Ops:
  6.5 88.2 %reduce-scatter.5.cloned.1.call-start = ((), (), s32[]{:S(2)}) async-start(), calls=%async_computation.4 | async-start | bytes 2621440 | tf_op jit(solution)/shard_map/reduce_scatter | solution.py:114
  9.2 53.4 %copy-start.2 = (bf16[1,1024,1024]{2,1,0:T(8,128)(2,1)S(1)}, bf16[1,1024,1024]{2,1,0:T(8,128)(2,1)}, u32[]{:S(2)}) copy-start(bf16[1,1024,1024]{2,1,0:T(8,128)(2,1)} %param.3) | copy-start | bytes 6291460
  9.2 27.2 %collective-permute-start.3 = (bf16[256,1024]{1,0:T(8,128)(2,1)S(1)}, bf16[256,1024]{1,0:T(8,128)(2,1)S(1)}, u32[]{:S(2)}, u32[]{:S(2)}) collective-permute-start(bf16[256,1024]{1,0:T(8,128)(2,1)S(1)} %get-tuple-element.41), channel_id=1, source_target_pairs={{0,16},{8,24},{16,0},{24,8},{1,17},{9,25},{17,1},{25,9},{2,18},{10... | collective-permute-start | bytes 1572872 | tf_op jit(solution)/shard_map/ppermute | solution.py:13
  36.4 13.1 %collective-permute-start.4 = (bf16[256,1024]{1,0:T(8,128)(2,1)S(1)}, bf16[256,1024]{1,0:T(8,128)(2,1)S(1)}, u32[]{:S(2)}, u32[]{:S(2)}) collective-permute-start(bf16[256,1024]{1,0:T(8,128)(2,1)S(1)} %collective-permute-done.3), channel_id=1, source_target_pairs={{0,1},{1,0},{2,3},{3,2},{4,5},{5,4},{6,7},{7,6},{8,9},{9,8},{10,11... | collective-permute-start | bytes 1572872 | tf_op jit(solution)/shard_map/ppermute | solution.py:13
  38.0 24.7 %collective-permute-start.2 = (bf16[256,1024]{1,0:T(8,128)(2,1)S(1)}, bf16[256,1024]{1,0:T(8,128)(2,1)S(1)}, u32[]{:S(2)}, u32[]{:S(2)}) collective-permute-start(bf16[256,1024]{1,0:T(8,128)(2,1)S(1)} %get-tuple-element.42), channel_id=1, source_target_pairs={{0,16},{8,24},{16,0},{24,8},{1,17},{9,25},{17,1},{25,9},{2,18},{10... | collective-permute-start | bytes 1572872 | tf_op jit(solution)/shard_map/ppermute | solution.py:13
  65.3 0.9 copy-start.8
  65.3 2.7 copy-start.7
  65.3 63.1 %all-gather.5.cloned.1.call-start = ((), (), s32[]{:S(2)}) async-start(), calls=%async_computation.5 | async-start | bytes 1310720 | tf_op jit(solution)/shard_map/all_gather | solution.py:123
  65.4 12.1 %collective-permute-start.5 = (bf16[256,1024]{1,0:T(8,128)(2,1)S(1)}, bf16[256,1024]{1,0:T(8,128)(2,1)}, u32[]{:S(2)}, u32[]{:S(2)}) collective-permute-start(bf16[256,1024]{1,0:T(8,128)(2,1)S(1)} %collective-permute-done.2), channel_id=1, source_target_pairs={{0,1},{1,0},{2,3},{3,2},{4,5},{5,4},{6,7},{7,6},{8,9},{9,8},{10,11... | collective-permute-start | bytes 1572872 | tf_op jit(solution)/shard_map/ppermute | solution.py:13
  66.2 24.2 %collective-permute-start.1 = (bf16[256,1024]{1,0:T(8,128)(2,1)}, bf16[256,1024]{1,0:T(8,128)(2,1)S(1)}, u32[]{:S(2)}, u32[]{:S(2)}) collective-permute-start(bf16[256,1024]{1,0:T(8,128)(2,1)} %get-tuple-element.43), channel_id=1, source_target_pairs={{0,16},{8,24},{16,0},{24,8},{1,17},{9,25},{17,1},{25,9},{2,18},{10... | collective-permute-start | bytes 1572872 | tf_op jit(solution)/shard_map/ppermute | solution.py:13
  90.4 10.6 %copy-start.6 = (bf16[256,1024]{1,0:T(8,128)(2,1)}, bf16[256,1024]{1,0:T(8,128)(2,1)S(1)}, u32[]{:S(2)}) copy-start(bf16[256,1024]{1,0:T(8,128)(2,1)S(1)} %collective-permute-done.1) | copy-start | bytes 1572868
  96.6 51.2 %reduce-scatter.7.cloned.1.call-start = ((), (), s32[]{:S(2)}) async-start(), calls=%async_computation.6 | async-start | bytes 2621440 | tf_op jit(solution)/shard_map/reduce_scatter | solution.py:114
  100.9 68.2 %all-gather.7.cloned.1.call-start = ((), (), s32[]{:S(2)}) async-start(), calls=%async_computation.7 | async-start | bytes 1310720 | tf_op jit(solution)/shard_map/all_gather | solution.py:123
  101.0 13.8 %collective-permute-start.6 = (bf16[256,1024]{1,0:T(8,128)(2,1)S(1)}, bf16[256,1024]{1,0:T(8,128)(2,1)S(1)}, u32[]{:S(2)}, u32[]{:S(2)}) collective-permute-start(bf16[256,1024]{1,0:T(8,128)(2,1)S(1)} %collective-permute-done.1), channel_id=1, source_target_pairs={{0,1},{1,0},{2,3},{3,2},{4,5},{5,4},{6,7},{7,6},{8,9},{9,8},{10,11... | collective-permute-start | bytes 1572872 | tf_op jit(solution)/shard_map/ppermute | solution.py:13
  102.5 25.8 %collective-permute-start = (bf16[256,1024]{1,0:T(8,128)(2,1)}, bf16[256,1024]{1,0:T(8,128)(2,1)}, u32[]{:S(2)}, u32[]{:S(2)}) collective-permute-start(bf16[256,1024]{1,0:T(8,128)(2,1)} %get-tuple-element.44), channel_id=1, source_target_pairs={{0,16},{8,24},{16,0},{24,8},{1,17},{9,25},{17,1},{25,9},{2,18},{10... | collective-permute-start | bytes 1572872 | tf_op jit(solution)/shard_map/ppermute | solution.py:13
  149.7 50.9 %reduce-scatter.9.cloned.1.call-start = ((), (), s32[]{:S(2)}) async-start(), calls=%async_computation.8 | async-start | bytes 2621440 | tf_op jit(solution)/shard_map/reduce_scatter | solution.py:114
  154.0 65.5 %all-gather.9.cloned.1.call-start = ((), (), s32[]{:S(2)}) async-start(), calls=%async_computation.9 | async-start | bytes 1310720 | tf_op jit(solution)/shard_map/all_gather | solution.py:123
  154.0 13.9 %collective-permute-start.7 = (bf16[256,1024]{1,0:T(8,128)(2,1)}, bf16[256,1024]{1,0:T(8,128)(2,1)S(1)}, u32[]{:S(2)}, u32[]{:S(2)}) collective-permute-start(bf16[256,1024]{1,0:T(8,128)(2,1)} %collective-permute-done), channel_id=1, source_target_pairs={{0,1},{1,0},{2,3},{3,2},{4,5},{5,4},{6,7},{7,6},{8,9},{9,8},{10,11... | collective-permute-start | bytes 1572872 | tf_op jit(solution)/shard_map/ppermute | solution.py:13
  169.1 33.5 %copy-start.4 = (bf16[512,1024]{1,0:T(8,128)(2,1)}, bf16[512,1024]{1,0:T(8,128)(2,1)S(1)}, u32[]{:S(2)}) copy-start(bf16[512,1024]{1,0:T(8,128)(2,1)S(1)} %pad_maximum_fusion.3) | copy-start | bytes 3145732
  202.5 51.2 %reduce-scatter.11.cloned.1.call-start = ((), (), s32[]{:S(2)}) async-start(), calls=%async_computation.10 | async-start | bytes 2621440 | tf_op jit(solution)/shard_map/reduce_scatter | solution.py:114
  206.8 1.2 copy-start.3
  206.8 65.8 %all-gather.11.cloned.1.call-start = ((), (), s32[]{:S(2)}) async-start(), calls=%async_computation.11 | async-start | bytes 1310720 | tf_op jit(solution)/shard_map/all_gather | solution.py:123
  208.0 2.3 copy-start
  219.5 36.1 %copy-start.1 = (bf16[1024,512]{0,1:T(8,128)(2,1)S(1)}, bf16[1024,512]{0,1:T(8,128)(2,1)}, u32[]{:S(2)}) copy-start(bf16[1024,512]{0,1:T(8,128)(2,1)} %all-gather.9.cloned.1.call-done) | copy-start | bytes 3145732
  255.6 17.0 %copy-start.5 = (bf16[512,1024]{1,0:T(8,128)(2,1)S(1)}, bf16[512,1024]{1,0:T(8,128)(2,1)}, u32[]{:S(2)}) copy-start(bf16[512,1024]{1,0:T(8,128)(2,1)} %copy-done.4) | copy-start | bytes 3145732
Sparse Core Ops, SparseCore 0:
  65.4 29.2 reduce-scatter.4
  96.8 16.8 all-gather.4
  116.3 31.4 reduce-scatter.6
  149.8 16.8 all-gather.6
  169.1 31.4 reduce-scatter.8
  202.6 16.8 all-gather.8
  222.2 31.4 reduce-scatter.10
  255.7 16.8 all-gather.10
where the time goes:
time: 285 us
  waiting for transfers between devices  206 us (72%)
  matrix products  31.7 us (11%)
  between operations  14.8 us (5%)
  other arithmetic  14 us (5%)
  starting transfers between devices  12.4 us (4%)
  local copies, waits for them, and re-layouts  5.35 us (2%)
    ppermute x8, waiting for transfers between devices, shifted_2(): lax.ppermute(value, axis, [(i, (i + by) % count) for i in range(count)])  99 us
    reduce_scatter x4, waiting for transfers between devices, reduce(): lax.psum_scatter(partial, 'aux', scatter_dimension=0, tiled=True)  89.4 us
    all_gather x4, waiting for transfers between devices, amplitudes_of(): return lax.all_gather(amplitudes, 'aux', axis=0, tiled=True)  17.8 us
    dot_general x4, matrix products, paired_plan(): term = jnp.dot(gathered[c], blocks[c], preferred_element_type=jnp.float32)  16.5 us
    dot_general x4, matrix products, reduce(): jnp.einsum('aq,bq->ab', own, block, preferred_element_type=jnp.float32)  15.2 us
    ppermute x8, starting transfers between devices, shifted_2(): lax.ppermute(value, axis, [(i, (i + by) % count) for i in range(count)])  11.9 us
    convert_element_type x4, other arithmetic, amplitudes_of(): (summed / (pair_level - row_level[:, None] - col_level[None, :])).astype(...  7.58 us
  transfers between devices with their start and end apart: 16, of which 14 were waited for; matrix products, arithmetic and copies ran while one was open for 11% of the time, Pallas kernels for 0%

commit v1 on v0

--- a/solution.py
+++ b/solution.py
@@ -6,6 +6,18 @@
 CHUNKS = 4
 AUX_BY_PERMUTE = False
 Z_GATED = False
+
+
+def collect(x, axis, dim):
+    ways, here, lap = (lax.axis_size(axis), lax.axis_index(axis), x.shape[dim])
+    line, have = (x, 1)
+    while have < ways:
+        line = jnp.concatenate(
+            [line, lax.ppermute(line, axis, [(d, (d - have) % ways) for d in range(ways)])],
+            axis=dim,
+        )
+        have = 2 * have
+    return jnp.roll(line, here * lap, axis=dim)
 
 
 def shifted_2(value, axis, by):
@@ -120,7 +132,7 @@
         )
         if AUX_BY_PERMUTE:
             return aux_all_gather(amplitudes)
-        return lax.all_gather(amplitudes, "aux", axis=0, tiled=True)
+        return collect(amplitudes, "aux", 0)
 
     arrived = [None] * CHUNKS
     blocks = [None] * CHUNKS

time: 285 us -> 239 us (0.84)
  waiting for transfers between devices: 206 us -> 157 us
  starting transfers between devices: 12.4 us -> 19.1 us
  matrix products: 31.7 us -> 26.1 us
    reduce_scatter x4, waiting for transfers between devices: 89.4 us -> 25.4 us  [reduce(): lax.psum_scatter(partial, 'aux', scatter_dimension=0, tiled=True)]
    ppermute x0 -> x8, waiting for transfers between devices: none -> 40.9 us  [collect(): lax.ppermute(line, axis, [(d, (d - have) % ways) for d in range(ways)])]
    all_gather x4 -> x0, waiting for transfers between devices: 17.8 us -> none  [amplitudes_of(): return lax.all_gather(amplitudes, 'aux', axis=0, tiled=True)]
    ppermute x8, waiting for transfers between devices: 99 us -> 90.4 us  [shifted_2(): lax.ppermute(value, axis, [(i, (i + by) % count) for i in range(count)])]
    ppermute x0 -> x8, starting transfers between devices: none -> 7.12 us  [collect(): lax.ppermute(line, axis, [(d, (d - have) % ways) for d in range(ways)])]
    concatenate x0 -> x8, other arithmetic: none -> 4.98 us  [the longest x4 4.84 us: collect(): return jnp.roll(line, here * lap, axis=dim)]
    dot_general x4, matrix products: 16.5 us -> 12.2 us  [paired_plan(): term = jnp.dot(gathered[c], blocks[c], preferred_element_type=jnp.float32)]
    convert_element_type x4, other arithmetic: 7.58 us -> 3.69 us  [amplitudes_of(): (summed / (pair_level - row_level[:, None] - col_level[None, :])).astype(...]
  transfers between devices with their start and end apart: 16 -> 20, of which waited for: 14 -> 19; matrix products, arithmetic and copies ran while one was open for 11% -> 10% of each run, Pallas kernels for 0% -> 0%
where the time goes in v1:
time: 239 us
  waiting for transfers between devices  157 us (66%)
  matrix products  26.1 us (11%)
  starting transfers between devices  19.1 us (8%)
  other arithmetic  16.1 us (7%)
  between operations  14.5 us (6%)
  local copies, waits for them, and re-layouts  5.93 us (2%)
    ppermute x8, waiting for transfers between devices, shifted_2(): lax.ppermute(value, axis, [(i, (i + by) % count) for i in range(count)])  90.4 us
    ppermute x8, waiting for transfers between devices, collect(): lax.ppermute(line, axis, [(d, (d - have) % ways) for d in range(ways)])  40.9 us
    reduce_scatter x4, waiting for transfers between devices, reduce(): lax.psum_scatter(partial, 'aux', scatter_dimension=0, tiled=True)  25.4 us
    dot_general x4, matrix products, reduce(): jnp.einsum('aq,bq->ab', own, block, preferred_element_type=jnp.float32)  13.9 us
    dot_general x4, matrix products, paired_plan(): term = jnp.dot(gathered[c], blocks[c], preferred_element_type=jnp.float32)  12.2 us
    ppermute x8, starting transfers between devices, shifted_2(): lax.ppermute(value, axis, [(i, (i + by) % count) for i in range(count)])  11.8 us
    ppermute x8, starting transfers between devices, collect(): lax.ppermute(line, axis, [(d, (d - have) % ways) for d in range(ways)])  7.12 us
    concatenate x4, other arithmetic, collect(): return jnp.roll(line, here * lap, axis=dim)  4.84 us
  transfers between devices with their start and end apart: 20, of which 19 were waited for; matrix products, arithmetic and copies ran while one was open for 10% of the time, Pallas kernels for 0%

profile of v1, /device:TPU:0, one launch (start us, length us, event | category | flops | bytes accessed | tf_op | source)
XLA Modules:
  0.0 238.5 jit_solution(9269684696717142671)
XLA Ops:
  6.5 2.8 %slice_bitcast_fusion = (bf16[256,1024]{1,0:T(8,128)(2,1)S(1)}, bf16[256,1024]{1,0:T(8,128)(2,1)S(1)}, bf16[256,1024]{1,0:T(8,128)(2,1)}, bf16[256,1024]{1,0:T(8,128)(2,1)}) fusion(bf16[1,1024,1024]{2,1,0:T(8,128)(2,1)} %param.5), kind=kLoop, calls=%fused_computation.71 | loop fusion | bytes 4194304 | tf_op jit(solution)/shard_map/slice | solution.py:145
  9.3 4.0 %collective-permute-start.3 = (bf16[256,1024]{1,0:T(8,128)(2,1)S(1)}, bf16[256,1024]{1,0:T(8,128)(2,1)S(1)}, u32[]{:S(2)}, u32[]{:S(2)}) collective-permute-start(bf16[256,1024]{1,0:T(8,128)(2,1)S(1)} %get-tuple-element.42), channel_id=1, source_target_pairs={{0,16},{8,24},{16,0},{24,8},{1,17},{9,25},{17,1},{25,9},{2,18},{10... | collective-permute-start | bytes 1572872 | tf_op jit(solution)/shard_map/ppermute | solution.py:25
  13.3 23.2 %collective-permute-done.3 = bf16[256,1024]{1,0:T(8,128)(2,1)S(1)} collective-permute-done((bf16[256,1024]{1,0:T(8,128)(2,1)S(1)}, bf16[256,1024]{1,0:T(8,128)(2,1)S(1)}, u32[]{:S(2)}, u32[]{:S(2)}) %collective-permute-start.3) | collective-permute-done | bytes 524320 | tf_op jit(solution)/shard_map/ppermute | solution.py:25
  38.1 11.5 %collective-permute-done.4 = bf16[256,1024]{1,0:T(8,128)(2,1)S(1)} collective-permute-done((bf16[256,1024]{1,0:T(8,128)(2,1)S(1)}, bf16[256,1024]{1,0:T(8,128)(2,1)S(1)}, u32[]{:S(2)}, u32[]{:S(2)}) %collective-permute-start.4) | collective-permute-done | bytes 524320 | tf_op jit(solution)/shard_map/ppermute | solution.py:25
  49.7 13.2 %collective-permute-done.2 = bf16[256,1024]{1,0:T(8,128)(2,1)} collective-permute-done((bf16[256,1024]{1,0:T(8,128)(2,1)S(1)}, bf16[256,1024]{1,0:T(8,128)(2,1)}, u32[]{:S(2)}, u32[]{:S(2)}) %collective-permute-start.2) | collective-permute-done | bytes 524320 | tf_op jit(solution)/shard_map/ppermute | solution.py:25
  62.8 2.6 %fusion.8 = f32[1024,512]{0,1:T(8,128)} fusion(bf16[512,1024]{1,0:T(8,128)(2,1)S(1)} %pad_maximum_fusion, bf16[1,1024,1024]{2,1,0:T(8,128)(2,1)S(1)} %copy-done.2), kind=kOutput, calls=%fused_computation.34 | convolution fusion | flops 1073741824 | bytes 5242880 | tf_op jit(solution)/shard_map/aq,bq->ab/dot_general | solution.py:123
  66.3 11.3 %collective-permute-done.5 = bf16[256,1024]{1,0:T(8,128)(2,1)S(1)} collective-permute-done((bf16[256,1024]{1,0:T(8,128)(2,1)}, bf16[256,1024]{1,0:T(8,128)(2,1)S(1)}, u32[]{:S(2)}, u32[]{:S(2)}) %collective-permute-start.5) | collective-permute-done | bytes 524320 | tf_op jit(solution)/shard_map/ppermute | solution.py:25
  78.8 11.8 %collective-permute-done.1 = bf16[256,1024]{1,0:T(8,128)(2,1)} collective-permute-done((bf16[256,1024]{1,0:T(8,128)(2,1)}, bf16[256,1024]{1,0:T(8,128)(2,1)}, u32[]{:S(2)}, u32[]{:S(2)}) %collective-permute-start.1) | collective-permute-done | bytes 524320 | tf_op jit(solution)/shard_map/ppermute | solution.py:25
  90.6 4.3 %reduce-scatter.5.cloned.1.call-done = f32[256,512]{0,1:T(8,128)} async-done(((f32[1024,512]{0,1:T(8,128)}), f32[256,512]{0,1:T(8,128)}) %reduce-scatter.5.cloned.1.call-update) | async-done | bytes 524304 | tf_op jit(solution)/shard_map/reduce_scatter | solution.py:126
  94.9 2.6 %fusion.11 = f32[1024,512]{0,1:T(8,128)} fusion(bf16[512,1024]{1,0:T(8,128)(2,1)S(1)} %pad_maximum_fusion.1, bf16[1,1024,1024]{2,1,0:T(8,128)(2,1)S(1)} %copy-done.2), kind=kOutput, calls=%fused_computation.35 | convolution fusion | flops 1073741824 | bytes 5242880 | tf_op jit(solution)/shard_map/aq,bq->ab/dot_general | solution.py:123
  101.9 2.3 collective-permute-done.7
  106.5 2.4 collective-permute-start
  108.9 6.0 %collective-permute-done.6 = bf16[256,1024]{1,0:T(8,128)(2,1)S(1)} collective-permute-done((bf16[256,1024]{1,0:T(8,128)(2,1)}, bf16[256,1024]{1,0:T(8,128)(2,1)S(1)}, u32[]{:S(2)}, u32[]{:S(2)}) %collective-permute-start.6) | collective-permute-done | bytes 524320 | tf_op jit(solution)/shard_map/ppermute | solution.py:25
  116.0 6.6 %collective-permute-done.8 = bf16[512,512]{0,1:T(8,128)(2,1)} collective-permute-done((bf16[512,512]{0,1:T(8,128)(2,1)S(1)}, bf16[512,512]{0,1:T(8,128)(2,1)}, u32[]{:S(2)}, u32[]{:S(2)}) %collective-permute-start.8) | collective-permute-done | bytes 524320 | tf_op jit(solution)/shard_map/ppermute | solution.py:16
  122.6 2.0 fusion.38
  124.6 9.0 %collective-permute-done = bf16[256,1024]{1,0:T(8,128)(2,1)} collective-permute-done((bf16[256,1024]{1,0:T(8,128)(2,1)}, bf16[256,1024]{1,0:T(8,128)(2,1)}, u32[]{:S(2)}, u32[]{:S(2)}) %collective-permute-start) | collective-permute-done | bytes 524320 | tf_op jit(solution)/shard_map/ppermute | solution.py:25
  133.6 4.2 %fusion.14 = f32[1024,512]{0,1:T(8,128)} fusion(bf16[512,1024]{1,0:T(8,128)(2,1)S(1)} %pad_maximum_fusion.2, bf16[1,1024,1024]{2,1,0:T(8,128)(2,1)} %param.5), kind=kOutput, calls=%fused_computation.36 | convolution fusion | flops 1073741824 | bytes 5242880 | tf_op jit(solution)/shard_map/aq,bq->ab/dot_general | solution.py:123
  140.7 2.4 %collective-permute-done.10 = bf16[256,512]{0,1:T(8,128)(2,1)S(1)} collective-permute-done((bf16[256,512]{0,1:T(8,128)(2,1)S(1)}, bf16[256,512]{0,1:T(8,128)(2,1)S(1)}, u32[]{:S(2)}, u32[]{:S(2)}) %collective-permute-start.10) | collective-permute-done | bytes 262176 | tf_op jit(solution)/shard_map/ppermute | solution.py:16
  144.7 4.6 %fusion.43 = f32[1024,1024]{1,0:T(8,128)} fusion(bf16[1024,512]{0,1:T(8,128)(2,1)S(1)} %fusion.38, bf16[512,1024]{1,0:T(8,128)(2,1)} %copy-done.1), kind=kOutput, calls=%fused_computation.82 | convolution fusion | flops 1073741824 | bytes 6291456 | tf_op jit(solution)/shard_map/dot_general | solution.py:186
  149.3 4.4 %collective-permute-done.9 = bf16[256,1024]{1,0:T(8,128)(2,1)S(1)} collective-permute-done((bf16[256,1024]{1,0:T(8,128)(2,1)}, bf16[256,1024]{1,0:T(8,128)(2,1)S(1)}, u32[]{:S(2)}, u32[]{:S(2)}) %collective-permute-start.9) | collective-permute-done | bytes 524320 | tf_op jit(solution)/shard_map/ppermute | solution.py:25
  153.7 2.1 pad_maximum_fusion.3
  155.8 2.9 %collective-permute-done.11 = bf16[512,512]{0,1:T(8,128)(2,1)S(1)} collective-permute-done((bf16[512,512]{0,1:T(8,128)(2,1)S(1)}, bf16[512,512]{0,1:T(8,128)(2,1)S(1)}, u32[]{:S(2)}, u32[]{:S(2)}) %collective-permute-start.11) | collective-permute-done | bytes 524320 | tf_op jit(solution)/shard_map/ppermute | solution.py:16
  159.7 10.7 %reduce-scatter.9.cloned.1.call-done = f32[256,512]{0,1:T(8,128)} async-done(((f32[1024,512]{0,1:T(8,128)}), f32[256,512]{0,1:T(8,128)}) %reduce-scatter.9.cloned.1.call-update) | async-done | bytes 524304 | tf_op jit(solution)/shard_map/reduce_scatter | solution.py:126
  170.4 4.5 %fusion.17 = f32[1024,512]{0,1:T(8,128)} fusion(bf16[512,1024]{1,0:T(8,128)(2,1)} %pad_maximum_fusion.3, bf16[1,1024,1024]{2,1,0:T(8,128)(2,1)} %param.5), kind=kOutput, calls=%fused_computation.37 | convolution fusion | flops 1073741824 | bytes 5242880 | tf_op jit(solution)/shard_map/aq,bq->ab/dot_general | solution.py:123
  177.5 3.9 %collective-permute-done.12 = bf16[256,512]{0,1:T(8,128)(2,1)S(1)} collective-permute-done((bf16[256,512]{0,1:T(8,128)(2,1)S(1)}, bf16[256,512]{0,1:T(8,128)(2,1)S(1)}, u32[]{:S(2)}, u32[]{:S(2)}) %collective-permute-start.12) | collective-permute-done | bytes 262176 | tf_op jit(solution)/shard_map/ppermute | solution.py:16
  184.7 2.9 %add.128 = f32[1024,1024]{1,0:T(8,128)} add(f32[1024,1024]{1,0:T(8,128)S(1)} %copy-done, f32[1024,1024]{1,0:T(8,128)S(1)} %fusion.44) | non-fusion elementwise | flops 1048576 | bytes 12582912 | tf_op jit(solution)/shard_map/add | solution.py:187
  187.6 9.6 %collective-permute-done.13 = bf16[512,512]{0,1:T(8,128)(2,1)S(1)} collective-permute-done((bf16[512,512]{0,1:T(8,128)(2,1)S(1)}, bf16[512,512]{0,1:T(8,128)(2,1)S(1)}, u32[]{:S(2)}, u32[]{:S(2)}) %collective-permute-start.13) | collective-permute-done | bytes 524320 | tf_op jit(solution)/shard_map/ppermute | solution.py:16
  198.1 10.4 %reduce-scatter.11.cloned.1.call-done = f32[256,512]{0,1:T(8,128)} async-done(((f32[1024,512]{0,1:T(8,128)}), f32[256,512]{0,1:T(8,128)}) %reduce-scatter.11.cloned.1.call-update) | async-done | bytes 524304 | tf_op jit(solution)/shard_map/reduce_scatter | solution.py:126
  210.1 3.9 %collective-permute-done.14 = bf16[256,512]{0,1:T(8,128)(2,1)S(1)} collective-permute-done((bf16[256,512]{0,1:T(8,128)(2,1)S(1)}, bf16[256,512]{0,1:T(8,128)(2,1)S(1)}, u32[]{:S(2)}, u32[]{:S(2)}) %collective-permute-start.14) | collective-permute-done | bytes 262176 | tf_op jit(solution)/shard_map/ppermute | solution.py:16
  215.4 3.6 %convolution_add_fusion = f32[1024,1024]{1,0:T(8,128)S(1)} fusion(f32[1024,1024]{1,0:T(8,128)} %add.128, bf16[1024,512]{0,1:T(8,128)(2,1)S(1)} %fusion.28, bf16[512,1024]{1,0:T(8,128)(2,1)S(1)} %pad_maximum_fusion.2), kind=kOutput, calls=%fused_computation.1 | convolution fusion | flops 1074790400 | bytes 10485760 | tf_op jit(solution)/shard_map/dot_general | solution.py:186
  219.0 9.3 %collective-permute-done.15 = bf16[512,512]{0,1:T(8,128)(2,1)S(1)} collective-permute-done((bf16[512,512]{0,1:T(8,128)(2,1)S(1)}, bf16[512,512]{0,1:T(8,128)(2,1)S(1)}, u32[]{:S(2)}, u32[]{:S(2)}) %collective-permute-start.15) | collective-permute-done | bytes 524320 | tf_op jit(solution)/shard_map/ppermute | solution.py:16
  229.3 2.7 %fusion.20 = bf16[1,1024,1024]{2,1,0:T(8,128)(2,1)} fusion(f32[1024,1024]{1,0:T(8,128)S(1)} %convolution_add_fusion, bf16[1024,512]{0,1:T(8,128)(2,1)S(1)} %fusion.23, bf16[512,1024]{1,0:T(8,128)(2,1)S(1)} %copy-done.3), kind=kOutput, calls=%fused_computation.38 | convolution fusion | flops 1076887552 | bytes 8388608 | tf_op jit(solution)/shard_map/dot_general | solution.py:186
  (62 shorter events, 26.3 us)
Async XLA Ops:
  6.5 88.4 %reduce-scatter.5.cloned.1.call-start = ((), (), s32[]{:S(2)}) async-start(), calls=%async_computation.4 | async-start | bytes 2621440 | tf_op jit(solution)/shard_map/reduce_scatter | solution.py:126
  9.3 53.5 %copy-start.2 = (bf16[1,1024,1024]{2,1,0:T(8,128)(2,1)S(1)}, bf16[1,1024,1024]{2,1,0:T(8,128)(2,1)}, u32[]{:S(2)}) copy-start(bf16[1,1024,1024]{2,1,0:T(8,128)(2,1)} %param.5) | copy-start | bytes 6291460
  9.3 27.2 %collective-permute-start.3 = (bf16[256,1024]{1,0:T(8,128)(2,1)S(1)}, bf16[256,1024]{1,0:T(8,128)(2,1)S(1)}, u32[]{:S(2)}, u32[]{:S(2)}) collective-permute-start(bf16[256,1024]{1,0:T(8,128)(2,1)S(1)} %get-tuple-element.42), channel_id=1, source_target_pairs={{0,16},{8,24},{16,0},{24,8},{1,17},{9,25},{17,1},{25,9},{2,18},{10... | collective-permute-start | bytes 1572872 | tf_op jit(solution)/shard_map/ppermute | solution.py:25
  36.5 13.1 %collective-permute-start.4 = (bf16[256,1024]{1,0:T(8,128)(2,1)S(1)}, bf16[256,1024]{1,0:T(8,128)(2,1)S(1)}, u32[]{:S(2)}, u32[]{:S(2)}) collective-permute-start(bf16[256,1024]{1,0:T(8,128)(2,1)S(1)} %collective-permute-done.3), channel_id=1, source_target_pairs={{0,1},{1,0},{2,3},{3,2},{4,5},{5,4},{6,7},{7,6},{8,9},{9,8},{10,11... | collective-permute-start | bytes 1572872 | tf_op jit(solution)/shard_map/ppermute | solution.py:25
  38.1 24.8 %collective-permute-start.2 = (bf16[256,1024]{1,0:T(8,128)(2,1)S(1)}, bf16[256,1024]{1,0:T(8,128)(2,1)}, u32[]{:S(2)}, u32[]{:S(2)}) collective-permute-start(bf16[256,1024]{1,0:T(8,128)(2,1)S(1)} %get-tuple-element.43), channel_id=1, source_target_pairs={{0,16},{8,24},{16,0},{24,8},{1,17},{9,25},{17,1},{25,9},{2,18},{10... | collective-permute-start | bytes 1572872 | tf_op jit(solution)/shard_map/ppermute | solution.py:25
  49.7 16.7 %copy-start.1 = (bf16[512,1024]{1,0:T(8,128)(2,1)}, bf16[512,1024]{1,0:T(8,128)(2,1)S(1)}, u32[]{:S(2)}) copy-start(bf16[512,1024]{1,0:T(8,128)(2,1)S(1)} %pad_maximum_fusion) | copy-start | bytes 3145732
  65.5 68.1 %reduce-scatter.7.cloned.1.call-start = ((), (), s32[]{:S(2)}) async-start(), calls=%async_computation.5 | async-start | bytes 2621440 | tf_op jit(solution)/shard_map/reduce_scatter | solution.py:126
  65.5 12.2 %collective-permute-start.5 = (bf16[256,1024]{1,0:T(8,128)(2,1)}, bf16[256,1024]{1,0:T(8,128)(2,1)S(1)}, u32[]{:S(2)}, u32[]{:S(2)}) collective-permute-start(bf16[256,1024]{1,0:T(8,128)(2,1)} %collective-permute-done.2), channel_id=1, source_target_pairs={{0,1},{1,0},{2,3},{3,2},{4,5},{5,4},{6,7},{7,6},{8,9},{9,8},{10,11... | collective-permute-start | bytes 1572872 | tf_op jit(solution)/shard_map/ppermute | solution.py:25
  66.3 24.3 %collective-permute-start.1 = (bf16[256,1024]{1,0:T(8,128)(2,1)}, bf16[256,1024]{1,0:T(8,128)(2,1)}, u32[]{:S(2)}, u32[]{:S(2)}) collective-permute-start(bf16[256,1024]{1,0:T(8,128)(2,1)} %get-tuple-element.44), channel_id=1, source_target_pairs={{0,16},{8,24},{16,0},{24,8},{1,17},{9,25},{17,1},{25,9},{2,18},{10... | collective-permute-start | bytes 1572872 | tf_op jit(solution)/shard_map/ppermute | solution.py:25
  97.5 0.7 copy-start.8
  97.5 2.4 %copy-start.7 = (f32[2048]{0:T(1024)S(1)}, f32[2048]{0:T(1024)}, u32[]{:S(2)}) copy-start(f32[2048]{0:T(1024)} %param.7) | copy-start | bytes 24580
  97.5 2.6 %copy-start.6 = (f32[256,512]{0,1:T(8,128)S(1)}, f32[256,512]{0,1:T(8,128)}, u32[]{:S(2)}) copy-start(f32[256,512]{0,1:T(8,128)} %reduce-scatter.5.cloned.1.call-done) | copy-start | bytes 1572868
  97.5 72.8 %reduce-scatter.9.cloned.1.call-start = ((), (), s32[]{:S(2)}) async-start(), calls=%async_computation.6 | async-start | bytes 2621440 | tf_op jit(solution)/shard_map/reduce_scatter | solution.py:126
  100.2 3.9 %collective-permute-start.7 = (bf16[256,512]{0,1:T(8,128)(2,1)S(1)}, bf16[256,512]{0,1:T(8,128)(2,1)S(1)}, u32[]{:S(2)}, u32[]{:S(2)}) collective-permute-start(bf16[256,512]{0,1:T(8,128)(2,1)S(1)} %divide_convert_fusion.3), channel_id=1, source_target_pairs={{0,6},{2,0},{4,2},{6,4},{1,7},{3,1},{5,3},{7,5},{8,14},{10,8},{12,... | collective-permute-start | bytes 786440 | tf_op jit(solution)/shard_map/ppermute | solution.py:16
  100.3 14.6 %collective-permute-start.6 = (bf16[256,1024]{1,0:T(8,128)(2,1)}, bf16[256,1024]{1,0:T(8,128)(2,1)S(1)}, u32[]{:S(2)}, u32[]{:S(2)}) collective-permute-start(bf16[256,1024]{1,0:T(8,128)(2,1)} %collective-permute-done.1), channel_id=1, source_target_pairs={{0,1},{1,0},{2,3},{3,2},{4,5},{5,4},{6,7},{7,6},{8,9},{9,8},{10,11... | collective-permute-start | bytes 1572872 | tf_op jit(solution)/shard_map/ppermute | solution.py:25
  104.2 0.7 copy-start.4
  104.9 17.6 %collective-permute-start.8 = (bf16[512,512]{0,1:T(8,128)(2,1)S(1)}, bf16[512,512]{0,1:T(8,128)(2,1)}, u32[]{:S(2)}, u32[]{:S(2)}) collective-permute-start(bf16[512,512]{0,1:T(8,128)(2,1)S(1)} %pad_maximum_fusion.4), channel_id=1, source_target_pairs={{0,4},{2,6},{4,0},{6,2},{1,5},{3,7},{5,1},{7,3},{8,12},{10,14},{12... | collective-permute-start | bytes 1572872 | tf_op jit(solution)/shard_map/ppermute | solution.py:16
  106.5 27.1 %collective-permute-start = (bf16[256,1024]{1,0:T(8,128)(2,1)}, bf16[256,1024]{1,0:T(8,128)(2,1)}, u32[]{:S(2)}, u32[]{:S(2)}) collective-permute-start(bf16[256,1024]{1,0:T(8,128)(2,1)} %get-tuple-element.45), channel_id=1, source_target_pairs={{0,16},{8,24},{16,0},{24,8},{1,17},{9,25},{17,1},{25,9},{2,18},{10... | collective-permute-start | bytes 1572872 | tf_op jit(solution)/shard_map/ppermute | solution.py:25
  108.9 13.7 %copy-start.5 = (bf16[256,512]{0,1:T(8,128)(2,1)S(1)}, bf16[256,512]{0,1:T(8,128)(2,1)}, u32[]{:S(2)}) copy-start(bf16[256,512]{0,1:T(8,128)(2,1)} %copy-done.4) | copy-start | bytes 786436
  137.8 70.7 %reduce-scatter.11.cloned.1.call-start = ((), (), s32[]{:S(2)}) async-start(), calls=%async_computation.7 | async-start | bytes 2621440 | tf_op jit(solution)/shard_map/reduce_scatter | solution.py:126
  139.1 4.0 %collective-permute-start.10 = (bf16[256,512]{0,1:T(8,128)(2,1)S(1)}, bf16[256,512]{0,1:T(8,128)(2,1)S(1)}, u32[]{:S(2)}, u32[]{:S(2)}) collective-permute-start(bf16[256,512]{0,1:T(8,128)(2,1)S(1)} %divide_convert_fusion.2), channel_id=1, source_target_pairs={{0,6},{2,0},{4,2},{6,4},{1,7},{3,1},{5,3},{7,5},{8,14},{10,8},{12,... | collective-permute-start | bytes 786440 | tf_op jit(solution)/shard_map/ppermute | solution.py:16
  139.2 14.5 %collective-permute-start.9 = (bf16[256,1024]{1,0:T(8,128)(2,1)}, bf16[256,1024]{1,0:T(8,128)(2,1)S(1)}, u32[]{:S(2)}, u32[]{:S(2)}) collective-permute-start(bf16[256,1024]{1,0:T(8,128)(2,1)} %collective-permute-done), channel_id=1, source_target_pairs={{0,1},{1,0},{2,3},{3,2},{4,5},{5,4},{6,7},{7,6},{8,9},{9,8},{10,11... | collective-permute-start | bytes 1572872 | tf_op jit(solution)/shard_map/ppermute | solution.py:25
  143.2 15.6 %collective-permute-start.11 = (bf16[512,512]{0,1:T(8,128)(2,1)S(1)}, bf16[512,512]{0,1:T(8,128)(2,1)S(1)}, u32[]{:S(2)}, u32[]{:S(2)}) collective-permute-start(bf16[512,512]{0,1:T(8,128)(2,1)S(1)} %pad_maximum_fusion.5), channel_id=1, source_target_pairs={{0,4},{2,6},{4,0},{6,2},{1,5},{3,7},{5,1},{7,3},{8,12},{10,14},{12... | collective-permute-start | bytes 1572872 | tf_op jit(solution)/shard_map/ppermute | solution.py:16
  176.1 5.3 %collective-permute-start.12 = (bf16[256,512]{0,1:T(8,128)(2,1)S(1)}, bf16[256,512]{0,1:T(8,128)(2,1)S(1)}, u32[]{:S(2)}, u32[]{:S(2)}) collective-permute-start(bf16[256,512]{0,1:T(8,128)(2,1)S(1)} %divide_convert_fusion.1), channel_id=1, source_target_pairs={{0,6},{2,0},{4,2},{6,4},{1,7},{3,1},{5,3},{7,5},{8,14},{10,8},{12,... | collective-permute-start | bytes 786440 | tf_op jit(solution)/shard_map/ppermute | solution.py:16
  181.5 15.7 %collective-permute-start.13 = (bf16[512,512]{0,1:T(8,128)(2,1)S(1)}, bf16[512,512]{0,1:T(8,128)(2,1)S(1)}, u32[]{:S(2)}, u32[]{:S(2)}) collective-permute-start(bf16[512,512]{0,1:T(8,128)(2,1)S(1)} %pad_maximum_fusion.6), channel_id=1, source_target_pairs={{0,4},{2,6},{4,0},{6,2},{1,5},{3,7},{5,1},{7,3},{8,12},{10,14},{12... | collective-permute-start | bytes 1572872 | tf_op jit(solution)/shard_map/ppermute | solution.py:16
  182.1 2.6 %copy-start = (f32[1024,1024]{1,0:T(8,128)S(1)}, f32[1024,1024]{1,0:T(8,128)}, u32[]{:S(2)}) copy-start(f32[1024,1024]{1,0:T(8,128)} %fusion.43) | copy-start | bytes 12582916
  209.7 4.3 %collective-permute-start.14 = (bf16[256,512]{0,1:T(8,128)(2,1)S(1)}, bf16[256,512]{0,1:T(8,128)(2,1)S(1)}, u32[]{:S(2)}, u32[]{:S(2)}) collective-permute-start(bf16[256,512]{0,1:T(8,128)(2,1)S(1)} %divide_convert_fusion), channel_id=1, source_target_pairs={{0,6},{2,0},{4,2},{6,4},{1,7},{3,1},{5,3},{7,5},{8,14},{10,8},{12,... | collective-permute-start | bytes 786440 | tf_op jit(solution)/shard_map/ppermute | solution.py:16
  214.0 14.3 %collective-permute-start.15 = (bf16[512,512]{0,1:T(8,128)(2,1)S(1)}, bf16[512,512]{0,1:T(8,128)(2,1)S(1)}, u32[]{:S(2)}, u32[]{:S(2)}) collective-permute-start(bf16[512,512]{0,1:T(8,128)(2,1)S(1)} %pad_maximum_fusion.7), channel_id=1, source_target_pairs={{0,4},{2,6},{4,0},{6,2},{1,5},{3,7},{5,1},{7,3},{8,12},{10,14},{12... | collective-permute-start | bytes 1572872 | tf_op jit(solution)/shard_map/ppermute | solution.py:16
  219.0 10.3 %copy-start.3 = (bf16[512,1024]{1,0:T(8,128)(2,1)S(1)}, bf16[512,1024]{1,0:T(8,128)(2,1)}, u32[]{:S(2)}) copy-start(bf16[512,1024]{1,0:T(8,128)(2,1)} %pad_maximum_fusion.3) | copy-start | bytes 3145732
Sparse Core Ops, SparseCore 0:
  65.6 29.2 reduce-scatter.4
  97.7 34.4 reduce-scatter.6
  137.9 32.3 reduce-scatter.8
  175.0 33.4 reduce-scatter.10
